TPU v7x, 512 devices: a whole 4x8x8 slice. The times are simulated.
512 devices in a mesh: tm: 32 (over x, y), space: 16 (over z, core).
Axes of the slice: x: 4, y: 8, z: 8, core: 2. Of those that a mesh axis runs over, the one named last changes fastest.
Arguments:
- data: bfloat16 [4096, 131072], P('tm', 'space'), may hold values from -40 to 40
- weights: float32 [131072], P('space'), may hold values from 1 to 30
- freqs: int32 [32], replicated, may hold values from 0 to 32, as said below
- n_keep: int32 [32], replicated, may hold values from 1 to 64, as said below
Outputs:
- mode_field: bfloat16 [32, 2, 64, 131072], P('tm', None, None, 'space')
- energy: float32 [32], P('tm')
Inputs may be any that keep to these rules, and one draw needn't show every extreme that they name: `freqs`: 32 distinct bins, among them 0 and 32, in an order drawn from the seed. `n_keep`: some frequency keeps all 64 columns and another keeps one.
All inputs are finite; a program needn't handle non-finite values.
Results may differ from a plain program's by a relative error of at most 0.0052.
Values may be sent and summed in bfloat16 or wider, within the bound.
No kernel may reach another device: no remote copies, remote signals or barrier semaphores. Data moves between devices by JAX's collectives and lax.ppermute only.
A program may use at most 64 MiB of HBM per device.

v0:
```python
import jax
import jax.numpy as jnp
from jax import lax
from jax.sharding import PartitionSpec as P

NT = 64
NS_STEPS = 4


def spectra_table(freqs):
    time_int = jnp.arange(NT, dtype=jnp.int32)
    time_float = time_int.astype(jnp.float32)
    window = 0.5 - 0.5 * jnp.cos(2.0 * jnp.pi * time_float / NT)
    norm = jnp.sqrt(jnp.sum(window * window))
    wrapped = freqs[:, None] * time_int[None, :] % NT
    phase_angle = 2.0 * jnp.pi * wrapped.astype(jnp.float32) / NT
    real_rows = window[None, :] * jnp.cos(phase_angle) / norm
    imag_rows = -window[None, :] * jnp.sin(phase_angle) / norm
    return jnp.concatenate([real_rows, imag_rows], axis=0).astype(jnp.bfloat16)


def transform_blocks(dft_table, snapshots, freq_count):
    block_count = snapshots.shape[0] // NT
    point_count = snapshots.shape[1]
    block_view = snapshots.reshape(block_count, NT, point_count)
    spectra = jnp.einsum("rt,btp->rbp", dft_table, block_view, preferred_element_type=jnp.float32)
    return spectra.reshape(2, freq_count, block_count, point_count)


def gram_terms(spectra, point_weights, total_points):
    spectra_re = spectra[0]
    spectra_im = spectra[1]
    stacked = jnp.concatenate([spectra_re, spectra_im], axis=1)
    square = (
        jnp.einsum(
            "fip,fjp->fij",
            stacked * point_weights[None, None, :],
            stacked,
            precision=lax.Precision.HIGHEST,
        )
        / total_points
    )
    return square


def unfold_terms(summed, block_count):
    g_one = summed[:, :block_count, :block_count] + summed[:, block_count:, block_count:]
    g_two = summed[:, :block_count, block_count:] - summed[:, block_count:, :block_count]
    return (g_one, g_two)


def inverse_root(embedded):
    size_two = embedded.shape[1]
    frobenius = jnp.sqrt(jnp.sum(embedded * embedded, axis=(1, 2)) + 1e-06)
    identity = jnp.broadcast_to(jnp.eye(size_two, dtype=jnp.float32), embedded.shape)
    current = embedded / frobenius[:, None, None]
    result = identity
    for sweep in range(NS_STEPS):
        factor = 1.5 * identity - 0.5 * jnp.einsum(
            "fij,fjk->fik", result, current, precision=lax.Precision.HIGHEST
        )
        current = jnp.einsum("fij,fjk->fik", current, factor, precision=lax.Precision.HIGHEST)
        result = jnp.einsum("fij,fjk->fik", factor, result, precision=lax.Precision.HIGHEST)
    return result


def finish_modes(spectra, summed, kept_counts, block_count):
    g_one, g_two = unfold_terms(summed, block_count)
    embedded = jnp.concatenate(
        [jnp.concatenate([g_one, -g_two], axis=2), jnp.concatenate([g_two, g_one], axis=2)], axis=1
    )
    inv_root = inverse_root(embedded)
    z_top = inv_root[:, :block_count, :block_count]
    z_low = inv_root[:, block_count:, :block_count]
    spectra_re = spectra[0]
    spectra_im = spectra[1]
    mode_re = jnp.einsum(
        "fij,fip->fjp", z_top, spectra_re, precision=lax.Precision.HIGHEST
    ) - jnp.einsum("fij,fip->fjp", z_low, spectra_im, precision=lax.Precision.HIGHEST)
    mode_im = jnp.einsum(
        "fij,fip->fjp", z_top, spectra_im, precision=lax.Precision.HIGHEST
    ) + jnp.einsum("fij,fip->fjp", z_low, spectra_re, precision=lax.Precision.HIGHEST)
    kept_mask = jnp.arange(block_count, dtype=jnp.int32)[None, :] < kept_counts[:, None]
    both_parts = jnp.stack([mode_re, mode_im], axis=1)
    mode_field = jnp.where(
        kept_mask[:, None, :, None], both_parts, jnp.zeros_like(both_parts)
    ).astype(jnp.bfloat16)
    energy = jnp.trace(g_one, axis1=1, axis2=2) / block_count
    return (mode_field, energy)


def shards(data, weights, freqs, n_keep):
    tm_count = lax.axis_size("tm")
    freq_count = freqs.shape[0]
    points_here = data.shape[1]
    total_points = points_here * lax.axis_size("space")
    block_count = data.shape[0] // NT * tm_count
    dft_table = spectra_table(freqs)
    spectra = transform_blocks(dft_table, data, freq_count)
    regrouped = lax.all_to_all(spectra, "tm", split_axis=1, concat_axis=2, tiled=True)
    partial_value = gram_terms(regrouped, weights, total_points)
    summed = lax.psum(partial_value, "space")
    kept_counts = lax.dynamic_slice_in_dim(n_keep, lax.axis_index("tm"), 1)
    mode_field, energy = finish_modes(regrouped, summed, kept_counts, block_count)
    return (mode_field, energy)


def solution(mesh):
    placed = (P("tm", "space"), P("space"), P(), P())
    return jax.shard_map(
        shards,
        mesh=mesh,
        in_specs=placed,
        out_specs=(P("tm", None, None, "space"), P("tm")),
        check_vma=False,
    )
```

profile of v0, /device:TPU:1, one launch (start us, length us, event | category | flops | bytes accessed | tf_op | source)
XLA Modules:
  0.0 300.4 jit_solution(1019790081844584022)
XLA Ops:
  7.2 0.0 copy-start
  7.2 0.7 multiply_reduce_fusion
  8.6 0.8 divide_convert_fusion.1
  9.4 0.0 copy-done
  9.4 0.7 fusion.36
  10.1 5.2 %copy.10 = f32[2,32,2,8192]{3,2,0,1:T(2,128)} copy(f32[2,32,2,8192]{3,1,2,0:T(8,128)S(1)} %fusion.36) | data formatting | bytes 8388608 | tf_op jit(solution)/shard_map/rt,btp->rbp/dot_general | solution.py:26
  15.3 0.0 copy-start.4
  15.3 10.7 %all-to-all-start = ((f32[2,32,2,8192]{3,2,0,1:T(2,128)}), f32[2,32,2,8192]{3,2,0,1:T(2,128)}, u32[]{:S(2)}, u32[]{:S(2)}) async-start(f32[2,32,2,8192]{3,2,0,1:T(2,128)} %copy.10), calls=%async_computation | async-start | bytes 8388608 | tf_op jit(solution)/shard_map/all_to_all | solution.py:100
  26.1 0.0 all-reduce.2.cloned.1.call-start
  26.1 0.0 copy-done.4
  26.1 0.6 dynamic_slice.3
  26.7 92.0 %all-to-all-done = f32[2,32,2,8192]{3,2,0,1:T(2,128)} async-done(((f32[2,32,2,8192]{3,2,0,1:T(2,128)}), f32[2,32,2,8192]{3,2,0,1:T(2,128)}, u32[]{:S(2)}, u32[]{:S(2)}) %all-to-all-start) | async-done | bytes 4194336 | tf_op jit(solution)/shard_map/all_to_all | solution.py:100
  118.7 4.8 %fusion.35 = (f32[1,32,2,8192]{3,2,0,1:T(2,128)}, f32[1,32,2,8192]{3,2,0,1:T(2,128)}) fusion(f32[2,32,2,8192]{3,2,0,1:T(2,128)} %all-to-all-done), kind=kLoop, calls=%fused_computation.61 | loop fusion | bytes 8388608 | tf_op jit(solution)/shard_map/slice | solution.py:31
  123.5 5.2 %squeeze.8 = f32[1,64,8192]{2,0,1:T(1,128)} reshape(f32[1,32,2,8192]{3,2,0,1:T(2,128)} %get-tuple-element.6) | data formatting | bytes 4194304 | tf_op jit(solution)/shard_map/squeeze | solution.py:31
  128.7 3.7 %concatenate.53 = f32[64,8192]{1,0:T(8,128)} reshape(f32[1,32,2,8192]{3,2,0,1:T(2,128)} %get-tuple-element.6) | data formatting | bytes 4194304 | tf_op jit(solution)/shard_map/concatenate | solution.py:33
  132.4 5.2 %squeeze.9 = f32[1,64,8192]{2,0,1:T(1,128)} reshape(f32[1,32,2,8192]{3,2,0,1:T(2,128)} %get-tuple-element.7) | data formatting | bytes 4194304 | tf_op jit(solution)/shard_map/squeeze | solution.py:32
  137.6 3.6 %concatenate.54 = f32[64,8192]{1,0:T(8,128)} reshape(f32[1,32,2,8192]{3,2,0,1:T(2,128)} %get-tuple-element.7) | data formatting | bytes 4194304 | tf_op jit(solution)/shard_map/concatenate | solution.py:33
  141.3 0.0 copy-start.3
  141.3 12.4 %pad_maximum_fusion = f32[1,128,8192]{2,0,1:T(1,128)} fusion(f32[1,64,8192]{2,0,1:T(1,128)} %squeeze.9, f32[1,64,8192]{2,0,1:T(1,128)} %squeeze.8), kind=kLoop, calls=%fused_computation.8 | loop fusion | flops 1048576 | bytes 8388608 | tf_op jit(solution)/shard_map/concatenate | solution.py:33
  153.6 0.0 copy-done.3
  153.6 9.6 %fusion.16 = f32[1,128,128]{2,1,0:T(8,128)} fusion(f32[1,128,8192]{2,0,1:T(1,128)} %pad_maximum_fusion, f32[64,8192]{1,0:T(8,128)} %concatenate.54, f32[64,8192]{1,0:T(8,128)} %concatenate.53, f32[8192]{0:T(1024)S(1)} %copy-done.3), kind=kOutput, calls=%fused_computation.24 | convolution fusion | flops 1612726272 | bytes 8486912 | tf_op jit(solution)/shard_map/fip,fjp->fij/dot_general | solution.py:35
  163.2 0.0 all-reduce.2.cloned.1.call-update
  163.3 0.7 iota_compare_fusion.4
  163.9 110.4 %all-reduce.2.cloned.1.call-done = f32[1,128,128]{2,1,0:T(8,128)} async-done(((f32[1,128,128]{2,1,0:T(8,128)}), f32[1,128,128]{2,1,0:T(8,128)}) %all-reduce.2.cloned.1.call-update) | async-done | bytes 65552 | tf_op jit(solution)/shard_map/psum | solution.py:102
  274.3 1.5 fusion.34
  275.9 0.7 fusion.19
  276.6 0.1 maximum_bitcast_fusion
  277.3 0.0 copy-start.1
  277.3 0.2 fusion.12
  277.5 0.2 fusion.29
  277.7 0.2 fusion.20
  277.9 0.2 fusion.11
  278.1 0.2 fusion.38
  278.3 0.2 fusion.37
  278.6 0.2 fusion.10
  278.8 0.2 fusion.40
  279.0 0.2 fusion.39
  279.2 0.2 fusion.9
  279.4 0.2 convolution_bitcast_fusion
  279.6 0.0 copy-done.1
  279.6 0.0 copy-start.2
  279.6 2.2 fusion.22
  281.8 0.0 copy-done.2
  281.8 1.9 fusion.21
  283.7 2.0 fusion.1
  285.8 3.0 %fusion = bf16[1,1,64,8192]{3,2,1,0:T(8,128)(2,1)} fusion(f32[64,8192]{1,0:T(8,128)S(1)} %fusion.21, f32[64,8192]{1,0:T(8,128)S(1)} %copy-done.1, f32[1,128,128]{2,1,0:T(8,128)S(1)} %convolution_bitcast_fusion), kind=kOutput, calls=%fused_computation.1 | convolution fusion | flops 403701760 | bytes 5275648 | tf_op jit(solution)/shard_map/fij,fip->fjp/dot_general | solution.py:82
  289.4 3.0 fusion.5
  (2 shorter events, 0.1 us)
Async XLA Ops:
  7.2 2.2 copy-start
  15.3 10.8 %copy-start.4 = (s32[32]{0:T(128)S(1)}, s32[32]{0:T(128)}, u32[]{:S(2)}) copy-start(s32[32]{0:T(128)} %param.7) | copy-start | bytes 388
  15.3 103.4 %all-to-all-start = ((f32[2,32,2,8192]{3,2,0,1:T(2,128)}), f32[2,32,2,8192]{3,2,0,1:T(2,128)}, u32[]{:S(2)}, u32[]{:S(2)}) async-start(f32[2,32,2,8192]{3,2,0,1:T(2,128)} %copy.10), calls=%async_computation | async-start | bytes 8388608 | tf_op jit(solution)/shard_map/all_to_all | solution.py:100
  26.1 248.3 %all-reduce.2.cloned.1.call-start = ((), (), s32[]{:S(2)}) async-start(), calls=%async_computation.1 | async-start | bytes 131072 | tf_op jit(solution)/shard_map/psum | solution.py:102
  141.3 12.4 %copy-start.3 = (f32[8192]{0:T(1024)S(1)}, f32[8192]{0:T(1024)}, u32[]{:S(2)}) copy-start(f32[8192]{0:T(1024)} %param.5) | copy-start | bytes 98308
  277.3 2.3 copy-start.1
  279.6 2.2 copy-start.2
Sparse Core Ops, SparseCore 0:
  163.4 110.9 all-reduce.1
where the time goes:
time: 301 us; the launch traced here: 300 us
  waiting for transfers between devices  202 us (67%)
  local copies, waits for them, and re-layouts  28.4 us (9%)
  matrix products  21.6 us (7%)
  other arithmetic  19.8 us (7%)
  between operations  17.4 us (6%)
  starting transfers between devices  10.8 us (4%)
    psum x1, waiting for transfers between devices, shards(): summed = lax.psum(partial_value, 'space')  110 us
    all_to_all x1, waiting for transfers between devices, shards(): lax.all_to_all(spectra, 'tm', split_axis=1, concat_axis=2, tiled=True)  92 us
    concatenate x1, other arithmetic, gram_terms(): stacked = jnp.concatenate([spectra_re, spectra_im], axis=1)  12.4 us
    all_to_all x1, starting transfers between devices, shards(): lax.all_to_all(spectra, 'tm', split_axis=1, concat_axis=2, tiled=True)  10.7 us
    dot_general x1, matrix products, gram_terms(): jnp.einsum('fip,fjp->fij', stacked * point_weights[None, None, :], stacke...  9.63 us
    concatenate x2, local copies, waits for them, and re-layouts, gram_terms(): stacked = jnp.concatenate([spectra_re, spectra_im], axis=1)  7.32 us
  transfers between devices with their start and end apart: 2, of which 2 were waited for; matrix products, arithmetic and copies ran while one was open for 0% of the time, Pallas kernels for 0%

commit v1 on v0

--- a/solution.py
+++ b/solution.py
@@ -99,7 +99,9 @@
     spectra = transform_blocks(dft_table, data, freq_count)
     regrouped = lax.all_to_all(spectra, "tm", split_axis=1, concat_axis=2, tiled=True)
     partial_value = gram_terms(regrouped, weights, total_points)
-    summed = lax.psum(partial_value, "space")
+    summed = partial_value
+    for hop in (1, 2, 4, 8):
+        summed = summed + lax.ppermute(summed, "space", [(dev, dev ^ hop) for dev in range(16)])
     kept_counts = lax.dynamic_slice_in_dim(n_keep, lax.axis_index("tm"), 1)
     mode_field, energy = finish_modes(regrouped, summed, kept_counts, block_count)
     return (mode_field, energy)

time: 301 us -> 203 us (0.67)
  waiting for transfers between devices: 202 us -> 4.84 us
  blocking collectives: 0 us -> 102 us
  starting transfers between devices: 10.8 us -> 25.2 us
  between operations: 17.4 us -> 3.98 us
  local copies, waits for them, and re-layouts: 28.4 us -> 24 us
    psum x1 -> x0, waiting for transfers between devices: 110 us -> none  [shards(): summed = lax.psum(partial_value, 'space')]
    all_to_all x0 -> x1, blocking collectives: none -> 102 us  [shards(): lax.all_to_all(spectra, 'tm', split_axis=1, concat_axis=2, tiled=True)]
    all_to_all x1 -> x0, waiting for transfers between devices: 92 us -> none  [shards(): lax.all_to_all(spectra, 'tm', split_axis=1, concat_axis=2, tiled=True)]
    ppermute x0 -> x4, starting transfers between devices: none -> 25.2 us  [shards(): lax.ppermute(summed, 'space', [(dev, dev ^ hop) for dev in range(16)])]
    all_to_all x1 -> x0, starting transfers between devices: 10.7 us -> none  [shards(): lax.all_to_all(spectra, 'tm', split_axis=1, concat_axis=2, tiled=True)]
    ppermute x0 -> x4, waiting for transfers between devices: none -> 4.84 us  [shards(): lax.ppermute(summed, 'space', [(dev, dev ^ hop) for dev in range(16)])]
  transfers between devices with their start and end apart: 2 -> 4, of which waited for: 2 -> 4; matrix products, arithmetic and copies ran while one was open for 0% -> 1% of each run, Pallas kernels for 0% -> 0%
where the time goes in v1:
time: 203 us; the launch traced here: 200 us
  blocking collectives  102 us (50%)
  starting transfers between devices  25.2 us (12%)
  local copies, waits for them, and re-layouts  24 us (12%)
  matrix products  20.8 us (10%)
  other arithmetic  19 us (9%)
  waiting for transfers between devices  4.84 us (2%)
  between operations  3.98 us (2%)
    all_to_all x1, blocking collectives, shards(): lax.all_to_all(spectra, 'tm', split_axis=1, concat_axis=2, tiled=True)  102 us
    ppermute x4, starting transfers between devices, shards(): lax.ppermute(summed, 'space', [(dev, dev ^ hop) for dev in range(16)])  25.2 us
    concatenate x1, other arithmetic, gram_terms(): stacked = jnp.concatenate([spectra_re, spectra_im], axis=1)  12.3 us
    dot_general x1, matrix products, gram_terms(): jnp.einsum('fip,fjp->fij', stacked * point_weights[None, None, :], stacke...  9.01 us
    concatenate x2, local copies, waits for them, and re-layouts, gram_terms(): stacked = jnp.concatenate([spectra_re, spectra_im], axis=1)  7.33 us
    squeeze x1, local copies, waits for them, and re-layouts, gram_terms(): spectra_re = spectra[0]  5.28 us
    squeeze x1, local copies, waits for them, and re-layouts, gram_terms(): spectra_im = spectra[1]  5.23 us
    ppermute x4, waiting for transfers between devices, shards(): lax.ppermute(summed, 'space', [(dev, dev ^ hop) for dev in range(16)])  4.84 us
  transfers between devices with their start and end apart: 4, of which 4 were waited for; matrix products, arithmetic and copies ran while one was open for 1% of the time, Pallas kernels for 0%

profile of v1, /device:TPU:1, one launch (start us, length us, event | category | flops | bytes accessed | tf_op | source)
XLA Modules:
  0.0 199.9 jit_solution(16664004244936908399)
XLA Ops:
  0.6 0.0 copy-start
  0.7 0.7 multiply_reduce_fusion
  2.0 0.8 divide_convert_fusion.1
  2.9 0.0 copy-done
  2.9 0.7 fusion.36
  3.6 3.2 %copy.10 = f32[2,32,2,8192]{3,2,0,1:T(2,128)S(1)} copy(f32[2,32,2,8192]{3,1,2,0:T(8,128)S(1)} %fusion.36) | data formatting | bytes 8388608 | tf_op jit(solution)/shard_map/rt,btp->rbp/dot_general | solution.py:26
  6.8 102.2 %all_to_all.4 = f32[2,32,2,8192]{3,2,0,1:T(2,128)S(1)} all-to-all(f32[2,32,2,8192]{3,2,0,1:T(2,128)S(1)} %copy.10), channel_id=1, replica_groups=mesh['tm'=32,'space'=16] {'tm'}, dimensions={1} | all-to-all | bytes 8388608 | tf_op jit(solution)/shard_map/all_to_all | solution.py:100
  109.0 2.3 %fusion.35 = (f32[1,32,2,8192]{3,2,0,1:T(2,128)}, f32[1,32,2,8192]{3,2,0,1:T(2,128)}) fusion(f32[2,32,2,8192]{3,2,0,1:T(2,128)S(1)} %all_to_all.4), kind=kLoop, calls=%fused_computation.61 | loop fusion | bytes 8388608 | tf_op jit(solution)/shard_map/slice | solution.py:31
  111.3 5.3 %squeeze.8 = f32[1,64,8192]{2,0,1:T(1,128)} reshape(f32[1,32,2,8192]{3,2,0,1:T(2,128)} %get-tuple-element.6) | data formatting | bytes 4194304 | tf_op jit(solution)/shard_map/squeeze | solution.py:31
  116.6 3.7 %concatenate.53 = f32[64,8192]{1,0:T(8,128)} reshape(f32[1,32,2,8192]{3,2,0,1:T(2,128)} %get-tuple-element.6) | data formatting | bytes 4194304 | tf_op jit(solution)/shard_map/concatenate | solution.py:33
  120.2 5.2 %squeeze.9 = f32[1,64,8192]{2,0,1:T(1,128)} reshape(f32[1,32,2,8192]{3,2,0,1:T(2,128)} %get-tuple-element.7) | data formatting | bytes 4194304 | tf_op jit(solution)/shard_map/squeeze | solution.py:32
  125.5 3.6 %concatenate.54 = f32[64,8192]{1,0:T(8,128)} reshape(f32[1,32,2,8192]{3,2,0,1:T(2,128)} %get-tuple-element.7) | data formatting | bytes 4194304 | tf_op jit(solution)/shard_map/concatenate | solution.py:33
  129.1 12.3 %pad_maximum_fusion = f32[1,128,8192]{2,0,1:T(1,128)} fusion(f32[1,64,8192]{2,0,1:T(1,128)} %squeeze.9, f32[1,64,8192]{2,0,1:T(1,128)} %squeeze.8), kind=kLoop, calls=%fused_computation.8 | loop fusion | flops 1048576 | bytes 8388608 | tf_op jit(solution)/shard_map/concatenate | solution.py:33
  141.5 0.0 copy-done.3
  141.5 9.0 %fusion.16 = f32[1,128,128]{2,1,0:T(8,128)S(1)} fusion(f32[1,128,8192]{2,0,1:T(1,128)} %pad_maximum_fusion, f32[64,8192]{1,0:T(8,128)} %concatenate.54, f32[64,8192]{1,0:T(8,128)} %concatenate.53, f32[8192]{0:T(1024)S(1)} %copy-done.3), kind=kOutput, calls=%fused_computation.24 | convolution fusion | flops 1612726272 | bytes 8486912 | tf_op jit(solution)/shard_map/fip,fjp->fij/dot_general | solution.py:35
  150.5 7.1 %collective-permute-start = (f32[1,128,128]{2,1,0:T(8,128)S(1)}, f32[1,128,128]{2,1,0:T(8,128)S(1)}, u32[]{:S(2)}, u32[]{:S(2)}) collective-permute-start(f32[1,128,128]{2,1,0:T(8,128)S(1)} %fusion.16), channel_id=1, source_target_pairs={{0,1},{1,0},{2,3},{3,2},{4,5},{5,4},{6,7},{7,6},{8,9},{9,8},{10,11... | collective-permute-start | bytes 196616 | tf_op jit(solution)/shard_map/ppermute | solution.py:104
  157.6 0.9 collective-permute-done
  158.5 4.0 %collective-permute-start.1 = (f32[1,128,128]{2,1,0:T(8,128)S(1)}, f32[1,128,128]{2,1,0:T(8,128)S(1)}, u32[]{:S(2)}, u32[]{:S(2)}) collective-permute-start(f32[1,128,128]{2,1,0:T(8,128)S(1)} %add.34), channel_id=1, source_target_pairs={{0,2},{1,3},{2,0},{3,1},{4,6},{5,7},{6,4},{7,5},{8,10},{9,11},{10,... | collective-permute-start | bytes 196616 | tf_op jit(solution)/shard_map/ppermute | solution.py:104
  162.5 2.1 %collective-permute-done.1 = f32[1,128,128]{2,1,0:T(8,128)S(1)} collective-permute-done((f32[1,128,128]{2,1,0:T(8,128)S(1)}, f32[1,128,128]{2,1,0:T(8,128)S(1)}, u32[]{:S(2)}, u32[]{:S(2)}) %collective-permute-start.1) | collective-permute-done | bytes 65568 | tf_op jit(solution)/shard_map/ppermute | solution.py:104
  164.6 5.8 %collective-permute-start.2 = (f32[1,128,128]{2,1,0:T(8,128)S(1)}, f32[1,128,128]{2,1,0:T(8,128)S(1)}, u32[]{:S(2)}, u32[]{:S(2)}) collective-permute-start(f32[1,128,128]{2,1,0:T(8,128)S(1)} %add.35), channel_id=1, source_target_pairs={{0,4},{1,5},{2,6},{3,7},{4,0},{5,1},{6,2},{7,3},{8,12},{9,13},{10,... | collective-permute-start | bytes 196616 | tf_op jit(solution)/shard_map/ppermute | solution.py:104
  170.5 0.0 copy-done.4
  170.5 0.6 dynamic_slice.3
  171.1 1.0 collective-permute-done.2
  172.1 8.2 %collective-permute-start.3 = (f32[1,128,128]{2,1,0:T(8,128)S(1)}, f32[1,128,128]{2,1,0:T(8,128)S(1)}, u32[]{:S(2)}, u32[]{:S(2)}) collective-permute-start(f32[1,128,128]{2,1,0:T(8,128)S(1)} %add.36), channel_id=1, source_target_pairs={{0,8},{1,9},{2,10},{3,11},{4,12},{5,13},{6,14},{7,15},{8,0},{9,1},... | collective-permute-start | bytes 196616 | tf_op jit(solution)/shard_map/ppermute | solution.py:104
  180.3 0.7 iota_compare_fusion.4
  181.0 0.8 collective-permute-done.3
  181.8 0.7 fusion.34
  182.5 0.7 fusion.19
  183.2 0.1 maximum_bitcast_fusion
  183.9 0.0 copy-start.1
  183.9 0.2 fusion.12
  184.1 0.2 fusion.29
  184.3 0.2 fusion.20
  184.5 0.2 fusion.11
  184.7 0.2 fusion.38
  184.9 0.2 fusion.37
  185.1 0.2 fusion.10
  185.3 0.2 fusion.40
  185.5 0.2 fusion.39
  185.8 0.2 fusion.9
  186.0 0.2 convolution_bitcast_fusion
  186.2 0.0 copy-done.1
  186.2 0.0 copy-start.2
  186.2 1.9 fusion.22
  188.1 1.9 fusion.21
  190.1 2.0 %fusion.1 = bf16[1,1,64,8192]{3,2,1,0:T(8,128)(2,1)S(1)} fusion(f32[64,8192]{1,0:T(8,128)S(1)} %fusion.22, f32[64,8192]{1,0:T(8,128)S(1)} %copy-done.2, f32[1,128,128]{2,1,0:T(8,128)S(1)} %convolution_bitcast_fusion), kind=kOutput, calls=%fused_computation.3 | convolution fusion | flops 403701760 | bytes 5275648 | tf_op jit(solution)/shard_map/fij,fip->fjp/dot_general | solution.py:79
  192.1 3.0 %fusion = bf16[1,1,64,8192]{3,2,1,0:T(8,128)(2,1)} fusion(f32[64,8192]{1,0:T(8,128)S(1)} %fusion.21, f32[64,8192]{1,0:T(8,128)S(1)} %copy-done.1, f32[1,128,128]{2,1,0:T(8,128)S(1)} %convolution_bitcast_fusion), kind=kOutput, calls=%fused_computation.1 | convolution fusion | flops 403701760 | bytes 5275648 | tf_op jit(solution)/shard_map/fij,fip->fjp/dot_general | solution.py:82
  195.8 3.0 %fusion.5 = bf16[1,2,64,8192]{3,2,1,0:T(8,128)(2,1)} fusion(bf16[1,1,64,8192]{3,2,1,0:T(8,128)(2,1)} %fusion, bf16[1,1,64,8192]{3,2,1,0:T(8,128)(2,1)S(1)} %fusion.1, pred[64]{0:T(512)(128)(4,1)S(1)} %iota_compare_fusion.4), kind=kLoop, calls=%fused_computation.10 | loop fusion | flops 5242880 | bytes 4194368 | tf_op jit(solution)/shard_map/convert_element_type | solution.py:87
  (9 shorter events, 0.1 us)
Async XLA Ops:
  0.6 2.2 %copy-start = (bf16[128,8192]{1,0:T(8,128)(2,1)S(1)}, bf16[128,8192]{1,0:T(8,128)(2,1)}, u32[]{:S(2)}) copy-start(bf16[128,8192]{1,0:T(8,128)(2,1)} %param.4) | copy-start | bytes 6291460
  129.1 12.3 %copy-start.3 = (f32[8192]{0:T(1024)S(1)}, f32[8192]{0:T(1024)}, u32[]{:S(2)}) copy-start(f32[8192]{0:T(1024)} %param.5) | copy-start | bytes 98308
  141.5 29.0 %copy-start.4 = (s32[32]{0:T(128)S(1)}, s32[32]{0:T(128)}, u32[]{:S(2)}) copy-start(s32[32]{0:T(128)} %param.7) | copy-start | bytes 388
  150.5 8.0 %collective-permute-start = (f32[1,128,128]{2,1,0:T(8,128)S(1)}, f32[1,128,128]{2,1,0:T(8,128)S(1)}, u32[]{:S(2)}, u32[]{:S(2)}) collective-permute-start(f32[1,128,128]{2,1,0:T(8,128)S(1)} %fusion.16), channel_id=1, source_target_pairs={{0,1},{1,0},{2,3},{3,2},{4,5},{5,4},{6,7},{7,6},{8,9},{9,8},{10,11... | collective-permute-start | bytes 196616 | tf_op jit(solution)/shard_map/ppermute | solution.py:104
  158.5 6.1 %collective-permute-start.1 = (f32[1,128,128]{2,1,0:T(8,128)S(1)}, f32[1,128,128]{2,1,0:T(8,128)S(1)}, u32[]{:S(2)}, u32[]{:S(2)}) collective-permute-start(f32[1,128,128]{2,1,0:T(8,128)S(1)} %add.34), channel_id=1, source_target_pairs={{0,2},{1,3},{2,0},{3,1},{4,6},{5,7},{6,4},{7,5},{8,10},{9,11},{10,... | collective-permute-start | bytes 196616 | tf_op jit(solution)/shard_map/ppermute | solution.py:104
  164.6 7.5 %collective-permute-start.2 = (f32[1,128,128]{2,1,0:T(8,128)S(1)}, f32[1,128,128]{2,1,0:T(8,128)S(1)}, u32[]{:S(2)}, u32[]{:S(2)}) collective-permute-start(f32[1,128,128]{2,1,0:T(8,128)S(1)} %add.35), channel_id=1, source_target_pairs={{0,4},{1,5},{2,6},{3,7},{4,0},{5,1},{6,2},{7,3},{8,12},{9,13},{10,... | collective-permute-start | bytes 196616 | tf_op jit(solution)/shard_map/ppermute | solution.py:104
  172.1 9.7 %collective-permute-start.3 = (f32[1,128,128]{2,1,0:T(8,128)S(1)}, f32[1,128,128]{2,1,0:T(8,128)S(1)}, u32[]{:S(2)}, u32[]{:S(2)}) collective-permute-start(f32[1,128,128]{2,1,0:T(8,128)S(1)} %add.36), channel_id=1, source_target_pairs={{0,8},{1,9},{2,10},{3,11},{4,12},{5,13},{6,14},{7,15},{8,0},{9,1},... | collective-permute-start | bytes 196616 | tf_op jit(solution)/shard_map/ppermute | solution.py:104
  183.9 2.3 %copy-start.1 = (f32[64,8192]{1,0:T(8,128)S(1)}, f32[64,8192]{1,0:T(8,128)}, u32[]{:S(2)}) copy-start(f32[64,8192]{1,0:T(8,128)} %concatenate.53) | copy-start | bytes 6291460
  186.2 1.9 copy-start.2
